TPU v7x, 128 devices: a whole 4x4x4 slice. The times are simulated.
128 devices in a mesh: ctx: 16 (over y_lo, z, core), head: 8 (over x, y_hi).
Axes of the slice: x: 4, y: 4 (y_hi: 2, y_lo: 2; y = y_hi * 2 + y_lo), z: 4, core: 2. Of those that a mesh axis runs over, the one named last changes fastest.
Arguments:
- hidden_in: bfloat16 [4096, 8192], P('ctx', 'head'), may hold values from -90 to 90
- query_rows: bfloat16 [4096, 8192], P('ctx', 'head'), may hold values from -5 to 5
- key_rows: bfloat16 [4096, 1024], P('ctx', 'head'), may hold values from -5 to 5
- value_rows: bfloat16 [4096, 1024], P('ctx', 'head'), may hold values from -6 to 6
- out_weight: bfloat16 [8192, 8192], P('head'), may hold values from -0.0625 to 0.0625
- grad_out: bfloat16 [4096, 8192], P('ctx', 'head'), may hold values from -6 to 6
- answer_mask: int32 [4096], P('ctx'), may hold values 0 or 1
Outputs:
- grad_query: bfloat16 [4096, 8192], P('ctx', 'head')
- grad_key: bfloat16 [4096, 1024], P('ctx', 'head')
- grad_value: bfloat16 [4096, 1024], P('ctx', 'head')
- fisher_q: float32 [16, 64], P('ctx', 'head')
- fisher_o: float32 [16, 64], P('ctx', 'head')
All inputs are finite; a program needn't handle non-finite values. No bound on the sum of `answer_mask` on one device may be relied on, other than what follows from the above.
Results may differ from a plain program's by a relative error of at most 0.019.
Values may be sent and summed in bfloat16 or wider, within the bound.
No kernel may reach another device: no remote copies, remote signals or barrier semaphores. Data moves between devices by JAX's collectives and lax.ppermute only.
A program may use at most 128 MiB of HBM per device.

v0:
```python
import math
import jax
import jax.numpy as jnp
from jax import lax
from jax.sharding import PartitionSpec as P

D = 8192
HEADS = 64
KVH = 8
HD = 128
NEGATIVE = -1e30
EPSILON = 1e-06


def block_scores(query_group, key_block, scaling, row_pos, col_pos):
    scores = (
        jnp.einsum("tgd,kd->tgk", query_group, key_block, preferred_element_type=jnp.float32)
        * scaling
    )
    return jnp.where(row_pos[:, None, None] >= col_pos[None, None, :], scores, NEGATIVE)


def head_squares(left_side, right_side, head_dim):
    product = lax.dot_general(
        left_side, right_side, (((0,), (0,)), ((), ())), preferred_element_type=jnp.float32
    )
    shaped = (product * product).reshape(
        product.shape[0], right_side.shape[1] // head_dim, head_dim
    )
    return jnp.sum(shaped, axis=(0, 2))


def body(hidden_in, query_rows, key_rows, value_rows, out_weight, grad_out, answer_mask):
    tok_dev = query_rows.shape[0]
    head_dim = HD
    group_size = HEADS // KVH
    local_groups = key_rows.shape[1] // head_dim
    scaling = head_dim ** (-0.5)
    own_index = lax.axis_index("ctx")
    first_row = own_index * tok_dev
    loss_weight = 0.25 + answer_mask.astype(jnp.float32)
    weighted = (grad_out.astype(jnp.float32) * loss_weight[:, None]).astype(jnp.bfloat16)
    keys_all, values_all = (
        lax.all_gather(key_rows, "ctx", axis=0, tiled=True),
        lax.all_gather(value_rows, "ctx", axis=0, tiled=True),
    )
    tokens = keys_all.shape[0]
    block_rows = math.gcd(512, tokens)

    def fetch(table, block_number):
        return lax.dynamic_slice_in_dim(table, block_number * block_rows, block_rows, 0)

    def column_pos(block_number):
        return block_number * block_rows + jnp.arange(block_rows, dtype=jnp.int32)

    buffer = jnp.zeros((tokens, 2 * local_groups * head_dim), jnp.float32)
    rows = query_rows.shape[0]
    row_pos = first_row + jnp.arange(rows, dtype=jnp.int32)
    needed = (first_row + rows - 1) // block_rows + 1
    query_heads = query_rows.reshape(rows, local_groups, group_size, head_dim)
    log_totals = []
    shared_head = 0
    query_group = query_heads[:, shared_head]

    def stats_step(block_number, carried):
        running_max, running_sum = carried
        key_block = fetch(keys_all, block_number)
        scores = block_scores(query_group, key_block, scaling, row_pos, column_pos(block_number))
        new_max = jnp.maximum(running_max, jnp.max(scores, axis=-1))
        running_sum = running_sum * jnp.exp(running_max - new_max) + jnp.sum(
            jnp.exp(scores - new_max[..., None]), axis=-1
        )
        return (new_max, running_sum)

    start_max = jnp.full((rows, group_size), NEGATIVE, jnp.float32)
    start_sum = jnp.zeros((rows, group_size), jnp.float32)
    running_max, running_sum = lax.fori_loop(0, needed, stats_step, (start_max, start_sum))
    log_total = running_max + jnp.log(running_sum)

    def value_step(block_number, accumulated):
        key_block = fetch(keys_all, block_number)
        value_block = fetch(values_all, block_number)
        scores = block_scores(query_group, key_block, scaling, row_pos, column_pos(block_number))
        rounded = jnp.exp(scores - log_total[..., None]).astype(jnp.bfloat16)
        return accumulated + jnp.einsum(
            "tgk,kd->tgd", rounded, value_block, preferred_element_type=jnp.float32
        )

    accumulated = lax.fori_loop(
        0, needed, value_step, jnp.zeros((rows, group_size, head_dim), jnp.float32)
    )
    log_totals.append(log_total)
    attended_list = [accumulated.astype(jnp.bfloat16)]
    attended_part = jnp.stack(attended_list, axis=1).reshape(
        rows, local_groups * group_size * head_dim
    )
    log_totals, attended = (log_totals, attended_part)
    piece_part = lax.all_gather(weighted, "head", axis=1, tiled=True)
    grad_sum = lax.dot_general(
        piece_part, out_weight, (((1,), (1,)), ((), ())), preferred_element_type=jnp.float32
    )
    grad_sum, squares_out = (grad_sum, head_squares(piece_part, attended, head_dim))
    grad_attended, squares_out = (grad_sum.astype(jnp.bfloat16), squares_out)
    backward_buffer = buffer
    rows = query_rows.shape[0]
    backward_row_pos = first_row + jnp.arange(rows, dtype=jnp.int32)
    needed = (first_row + rows - 1) // block_rows + 1
    query_heads = query_rows.reshape(rows, local_groups, group_size, head_dim)
    grad_heads = grad_attended.reshape(rows, local_groups, group_size, head_dim)
    attended_heads = attended.reshape(rows, local_groups, group_size, head_dim)
    shared_head = 0
    backward_query_group = query_heads[:, shared_head]
    grad_group = grad_heads[:, shared_head]
    backward_log_total = log_totals[shared_head]
    row_dot = jnp.sum(
        grad_group.astype(jnp.float32) * attended_heads[:, shared_head].astype(jnp.float32), axis=-1
    )
    key_column = jnp.int32(shared_head * head_dim)
    value_column = jnp.int32((local_groups + shared_head) * head_dim)

    def back_step(block_number, carried):
        query_sum, buffer_now = carried
        key_block = fetch(keys_all, block_number)
        value_block = fetch(values_all, block_number)
        scores = block_scores(
            backward_query_group, key_block, scaling, backward_row_pos, column_pos(block_number)
        )
        softmax = jnp.exp(scores - backward_log_total[..., None])
        rounded = softmax.astype(jnp.bfloat16)
        grad_prob = jnp.einsum(
            "tgd,kd->tgk", grad_group, value_block, preferred_element_type=jnp.float32
        )
        grad_score = (softmax * (grad_prob - row_dot[..., None]) * scaling).astype(jnp.bfloat16)
        query_sum = query_sum + jnp.einsum(
            "tgk,kd->tgd", grad_score, key_block, preferred_element_type=jnp.float32
        )
        key_part = jnp.einsum(
            "tgk,tgd->kd", grad_score, backward_query_group, preferred_element_type=jnp.float32
        )
        value_part = jnp.einsum(
            "tgk,tgd->kd", rounded, grad_group, preferred_element_type=jnp.float32
        )
        row_start = (block_number * block_rows).astype(jnp.int32)
        old_key = lax.dynamic_slice(buffer_now, (row_start, key_column), (block_rows, head_dim))
        buffer_now = lax.dynamic_update_slice(
            buffer_now, old_key + key_part, (row_start, key_column)
        )
        old_value = lax.dynamic_slice(buffer_now, (row_start, value_column), (block_rows, head_dim))
        buffer_now = lax.dynamic_update_slice(
            buffer_now, old_value + value_part, (row_start, value_column)
        )
        return (query_sum, buffer_now)

    start_query = jnp.zeros((rows, group_size, head_dim), jnp.float32)
    query_sum, backward_buffer = lax.fori_loop(0, needed, back_step, (start_query, backward_buffer))
    query_grads = [query_sum.astype(jnp.bfloat16)]
    grad_query_part = jnp.stack(query_grads, axis=1).reshape(
        rows, local_groups * group_size * head_dim
    )
    key_sums = lax.psum_scatter(
        backward_buffer.astype(jnp.bfloat16), "ctx", scatter_dimension=0, tiled=True
    ).astype(jnp.float32)
    grad_key = key_sums[:, : local_groups * head_dim].astype(jnp.bfloat16)
    grad_value = key_sums[:, local_groups * head_dim :].astype(jnp.bfloat16)
    squares_query = head_squares(
        lax.all_gather(hidden_in, "head", axis=1, tiled=True), grad_query_part, head_dim
    )
    normal_size = D * head_dim * tok_dev
    fisher_q = jnp.log(squares_query / normal_size + EPSILON).reshape(1, -1)
    fisher_o = jnp.log(squares_out / normal_size + EPSILON).reshape(1, -1)
    return (grad_query_part, grad_key, grad_value, fisher_q, fisher_o)


def solution(mesh):
    return jax.shard_map(
        body,
        mesh=mesh,
        in_specs=(
            P("ctx", "head"),
            P("ctx", "head"),
            P("ctx", "head"),
            P("ctx", "head"),
            P("head", None),
            P("ctx", "head"),
            P("ctx"),
        ),
        out_specs=(
            P("ctx", "head"),
            P("ctx", "head"),
            P("ctx", "head"),
            P("ctx", "head"),
            P("ctx", "head"),
        ),
        check_vma=False,
    )
```

profile of v0, /device:TPU:0, one launch (start us, length us, event | category | flops | bytes accessed | tf_op | source)
XLA Modules:
  0.0 331.3 jit_solution(14228058823165366588)
XLA Ops:
  7.2 0.0 all-gather.5.cloned.1.call-start
  7.2 0.7 all-gather.5.cloned.1.call-update
  7.9 0.0 all-gather.7.cloned.1.call-start
  7.9 0.7 all-gather.7.cloned.1.call-update
  8.7 0.0 all-gather.9.cloned.1.call-start
  8.7 0.7 convert_add_fusion
  9.4 2.0 multiply_convert_fusion
  11.4 0.0 all-gather.9.cloned.1.call-update
  11.4 0.0 all-gather.11.cloned.1.call-start
  11.4 0.5 all-gather.11.cloned.1.call-update
  12.0 0.0 reduce-scatter.2.cloned.1.call-start
  12.0 1.2 copy.28
  13.3 0.3 copy.33
  13.6 31.2 %all-gather.5.cloned.1.call-done = bf16[4096,128]{1,0:T(8,128)(2,1)} async-done(((bf16[256,128]{1,0:T(8,128)(2,1)}), bf16[4096,128]{1,0:T(8,128)(2,1)}) %all-gather.5.cloned.1.call-update) | async-done | bytes 1048592 | tf_op jit(solution)/shard_map/all_gather | solution.py:44
  44.8 2.8 while.37
  44.8 0.1 broadcast_compare_fusion.6
  44.9 1.7 fusion.94
  46.7 0.9 exponential_reduce_fusion.2
  47.6 31.5 %all-gather.7.cloned.1.call-done = bf16[4096,128]{1,0:T(8,128)(2,1)} async-done(((bf16[256,128]{1,0:T(8,128)(2,1)}), bf16[4096,128]{1,0:T(8,128)(2,1)}) %all-gather.7.cloned.1.call-update) | async-done | bytes 1048592 | tf_op jit(solution)/shard_map/all_gather | solution.py:45
  79.0 0.1 broadcast.135.clone
  79.1 2.9 while.38
  79.2 0.1 broadcast_compare_fusion.7
  79.3 2.7 fusion.98
  82.0 0.2 copy.32
  82.3 71.2 %all-gather.9.cloned.1.call-done = bf16[256,8192]{1,0:T(8,128)(2,1)} async-done(((bf16[256,1024]{1,0:T(8,128)(2,1)}), bf16[256,8192]{1,0:T(8,128)(2,1)}) %all-gather.9.cloned.1.call-update) | async-done | bytes 4194320 | tf_op jit(solution)/shard_map/all_gather | solution.py:98
  153.4 11.6 %convolution_convert_fusion = bf16[256,1024]{1,0:T(8,128)(2,1)S(1)} fusion(bf16[256,8192]{1,0:T(8,128)(2,1)} %all-gather.9.cloned.1.call-done, bf16[1024,8192]{1,0:T(8,128)(2,1)} %param.17), kind=kOutput, calls=%fused_computation.63 | convolution fusion | flops 4295229440 | bytes 21495808 | tf_op jit(solution)/shard_map/dot_general | solution.py:99
  165.0 0.1 copy_bitcast_fusion.1
  165.1 0.1 copy.40
  165.2 0.3 copy.30
  165.5 0.2 multiply_reduce_fusion.2
  165.7 0.1 broadcast.135
  165.8 2.2 broadcast_in_dim.48
  168.0 11.3 %while.39 = (s32[]{:T(128)}, f32[256,8,128]{2,0,1:T(8,128)S(1)}, f32[4096,256]{1,0:T(8,128)}, s32[]{:T(128)}, bf16[4096,128]{1,0:T(8,128)(2,1)}, /*index=5*/bf16...) while((s32[]{:T(128)}, f32[256,8,128]{2,0,1:T(8,128)S(1)}, ...), condition=%wide.region_8.9_spmd.clone, body=%wide.region_7.8_spmd.clone.sunk | while | flops 1354236672 | bytes 24934616 | solution.py:155
  168.0 0.1 broadcast_compare_fusion.8
  168.2 1.6 fusion.109
  169.8 2.4 fusion.110
  172.2 1.8 convolution_add_fusion.2
  174.1 2.4 fusion.111
  176.5 2.8 fusion.112
  179.3 3.8 %convert_element_type.47 = bf16[4096,256]{1,0:T(8,128)(2,1)} convert(f32[4096,256]{1,0:T(8,128)} %get-tuple-element.150) | non-fusion elementwise | flops 1048576 | bytes 6291456 | tf_op jit(solution)/shard_map/convert_element_type | solution.py:161
  183.0 0.0 reduce-scatter.2.cloned.1.call-update
  183.1 7.0 %multiply_reduce_fusion = f32[1024]{0:T(1024)S(1)} fusion(bf16[256,8192]{1,0:T(8,128)(2,1)} %all-gather.9.cloned.1.call-done, bf16[256,1024]{0,1:T(8,128)(2,1)S(1)} %bitcast.153), kind=kOutput, calls=%fused_computation.61 | convolution fusion | flops 4311743488 | bytes 4722688 | tf_op jit(solution)/shard_map/dot_general | solution.py:24
  190.1 0.1 bitcast_reduce_fusion
  190.2 0.1 copy_bitcast_fusion
  190.3 0.0 copy-start
  190.3 34.7 %all-gather.11.cloned.1.call-done = bf16[256,8192]{1,0:T(8,128)(2,1)} async-done(((bf16[256,1024]{1,0:T(8,128)(2,1)}), bf16[256,8192]{1,0:T(8,128)(2,1)}) %all-gather.11.cloned.1.call-update) | async-done | bytes 4194320 | tf_op jit(solution)/shard_map/all_gather | solution.py:166
  225.1 7.1 %multiply_reduce_fusion.1 = f32[1024]{0:T(1024)S(1)} fusion(bf16[256,1024]{1,0:T(8,128)(2,1)S(1)} %copy_bitcast_fusion, bf16[256,8192]{1,0:T(8,128)(2,1)} %all-gather.11.cloned.1.call-done), kind=kOutput, calls=%fused_computation.62 | convolution fusion | flops 4311743488 | bytes 4722688 | tf_op jit(solution)/shard_map/dot_general | solution.py:24
  232.2 0.0 copy-done
  232.2 0.1 bitcast_reduce_fusion.1
  232.3 0.5 log_bitcast_fusion
  232.8 0.5 log_bitcast_fusion.1
  233.4 89.9 %reduce-scatter.2.cloned.1.call-done = bf16[256,256]{1,0:T(8,128)(2,1)} async-done(((bf16[4096,256]{1,0:T(8,128)(2,1)}), bf16[256,256]{1,0:T(8,128)(2,1)}) %reduce-scatter.2.cloned.1.call-update) | async-done | bytes 131088 | tf_op jit(solution)/shard_map/reduce_scatter | solution.py:160
  323.3 1.5 fusion.57
  (12 shorter events, 0.0 us)
Async XLA Ops:
  7.2 37.6 %all-gather.5.cloned.1.call-start = ((), (), s32[]{:S(2)}) async-start(), calls=%async_computation.1 | async-start | bytes 1114112 | tf_op jit(solution)/shard_map/all_gather | solution.py:44
  7.9 71.1 %all-gather.7.cloned.1.call-start = ((), (), s32[]{:S(2)}) async-start(), calls=%async_computation.2 | async-start | bytes 1114112 | tf_op jit(solution)/shard_map/all_gather | solution.py:45
  8.7 144.8 %all-gather.9.cloned.1.call-start = ((), (), s32[]{:S(2)}) async-start(), calls=%async_computation.3 | async-start | bytes 4718592 | tf_op jit(solution)/shard_map/all_gather | solution.py:98
  11.4 213.7 %all-gather.11.cloned.1.call-start = ((), (), s32[]{:S(2)}) async-start(), calls=%async_computation.5 | async-start | bytes 4718592 | tf_op jit(solution)/shard_map/all_gather | solution.py:166
  12.0 311.3 %reduce-scatter.2.cloned.1.call-start = ((), (), s32[]{:S(2)}) async-start(), calls=%async_computation.4 | async-start | bytes 2228224 | tf_op jit(solution)/shard_map/reduce_scatter | solution.py:160
  190.3 41.9 %copy-start = (bf16[256,1024]{1,0:T(8,128)(2,1)}, bf16[256,1024]{1,0:T(8,128)(2,1)S(1)}, u32[]{:S(2)}) copy-start(bf16[256,1024]{1,0:T(8,128)(2,1)S(1)} %copy_bitcast_fusion) | copy-start | bytes 1572868
Sparse Core Ops, SparseCore 0:
  9.7 35.0 all-gather.4
  46.5 32.5 all-gather.6
  82.0 71.3 all-gather.8
  155.6 69.3 all-gather.10
  227.3 95.9 reduce-scatter.1
where the time goes:
time: 333 us; the launch traced here: 331 us
  waiting for transfers between devices  260 us (78%)
  matrix products  41.2 us (12%)
  between operations  13.9 us (4%)
  other arithmetic  9.25 us (3%)
  local copies, waits for them, and re-layouts  6.17 us (2%)
    reduce_scatter x1, waiting for transfers between devices, body(): lax.psum_scatter(backward_buffer.astype(jnp.bfloat16), 'ctx', scatter_dim...  89.9 us
    all_gather x1, waiting for transfers between devices, body(): piece_part = lax.all_gather(weighted, 'head', axis=1, tiled=True)  71.2 us
    all_gather x1, waiting for transfers between devices, body(): lax.all_gather(hidden_in, 'head', axis=1, tiled=True)  34.7 us
    all_gather x1, waiting for transfers between devices, body(): lax.all_gather(value_rows, 'ctx', axis=0, tiled=True)  31.5 us
    all_gather x1, waiting for transfers between devices, body(): lax.all_gather(key_rows, 'ctx', axis=0, tiled=True)  31.2 us
    dot_general x2, matrix products, head_squares(): lax.dot_general(left_side, right_side, (((0,), (0,)), ((), ())), preferre...  14.2 us
    dot_general x1, matrix products, body(): lax.dot_general(piece_part, out_weight, (((1,), (1,)), ((), ())), preferr...  11.6 us
  transfers between devices with their start and end apart: 5, of which 5 were waited for; matrix products, arithmetic and copies ran while one was open for 17% of the time, Pallas kernels for 0%

commit v1 on v0

--- a/solution.py
+++ b/solution.py
@@ -95,7 +95,9 @@
         rows, local_groups * group_size * head_dim
     )
     log_totals, attended = (log_totals, attended_part)
-    piece_part = lax.all_gather(weighted, "head", axis=1, tiled=True)
+    piece_part = jnp.concatenate(
+        lax.all_to_all(jnp.stack([weighted] * lax.axis_size("head")), "head", 0, 0), axis=1
+    )
     grad_sum = lax.dot_general(
         piece_part, out_weight, (((1,), (1,)), ((), ())), preferred_element_type=jnp.float32
     )

time: 333 us -> 317 us (0.952)
  waiting for transfers between devices: 260 us -> 236 us
  starting transfers between devices: 0.19 us -> 7.3 us
    all_gather x1 -> x0, waiting for transfers between devices: 71.2 us -> none  [body(): piece_part = lax.all_gather(weighted, 'head', axis=1, tiled=True)]
    reduce_scatter x1, waiting for transfers between devices: 89.9 us -> 113 us  [body(): lax.psum_scatter(backward_buffer.astype(jnp.bfloat16), 'ctx', scatter_dim...]
    all_gather x1, waiting for transfers between devices: 31.2 us -> 53.8 us  [body(): lax.all_gather(key_rows, 'ctx', axis=0, tiled=True)]
    all_to_all x0 -> x1, starting transfers between devices: none -> 7.15 us  [body(): lax.all_to_all(jnp.stack([weighted] * lax.axis_size('head')), 'head', 0, 0)]
  transfers between devices with their start and end apart: 5 -> 5, of which waited for: 5 -> 4; matrix products, arithmetic and copies ran while one was open for 17% -> 18% of each run, Pallas kernels for 0% -> 0%
where the time goes in v1:
time: 317 us; the launch traced here: 315 us
  waiting for transfers between devices  236 us (74%)
  matrix products  41.3 us (13%)
  between operations  13.9 us (4%)
  other arithmetic  8.46 us (3%)
  local copies, waits for them, and re-layouts  7.58 us (2%)
  starting transfers between devices  7.3 us (2%)
    reduce_scatter x1, waiting for transfers between devices, body(): lax.psum_scatter(backward_buffer.astype(jnp.bfloat16), 'ctx', scatter_dim...  113 us
    all_gather x1, waiting for transfers between devices, body(): lax.all_gather(key_rows, 'ctx', axis=0, tiled=True)  53.8 us
    all_gather x1, waiting for transfers between devices, body(): lax.all_gather(value_rows, 'ctx', axis=0, tiled=True)  34 us
    all_gather x1, waiting for transfers between devices, body(): lax.all_gather(hidden_in, 'head', axis=1, tiled=True)  33.1 us
    dot_general x2, matrix products, head_squares(): lax.dot_general(left_side, right_side, (((0,), (0,)), ((), ())), preferre...  14.1 us
    dot_general x1, matrix products, body(): lax.dot_general(piece_part, out_weight, (((1,), (1,)), ((), ())), preferr...  11.6 us
    all_to_all x1, starting transfers between devices, body(): lax.all_to_all(jnp.stack([weighted] * lax.axis_size('head')), 'head', 0, 0)  7.15 us
  transfers between devices with their start and end apart: 5, of which 4 were waited for; matrix products, arithmetic and copies ran while one was open for 18% of the time, Pallas kernels for 0%

profile of v1, /device:TPU:0, one launch (start us, length us, event | category | flops | bytes accessed | tf_op | source)
XLA Modules:
  0.0 315.0 jit_solution(2720503980437639266)
XLA Ops:
  7.2 0.0 all-gather.4.cloned.1.call-start
  7.2 0.7 all-gather.4.cloned.1.call-update
  7.9 0.0 all-gather.6.cloned.1.call-start
  7.9 0.7 all-gather.6.cloned.1.call-update
  8.6 0.7 convert_add_fusion
  9.3 1.2 multiply_convert_fusion
  10.5 0.2 copy.31
  10.7 2.2 stack.2
  13.0 0.0 copy-start.1
  13.0 7.1 %all-to-all-start = ((bf16[8,256,1024]{1,2,0:T(8,128)(2,1)}), bf16[8,256,1024]{1,2,0:T(8,128)(2,1)}, u32[]{:S(2)}, u32[]{:S(2)}) async-start(bf16[8,256,1024]{1,2,0:T(8,128)(2,1)} %stack.2), calls=%async_computation | async-start | bytes 8388608 | tf_op jit(solution)/shard_map/all_to_all | solution.py:99
  20.1 0.0 all-gather.8.cloned.1.call-start
  20.2 0.7 all-gather.8.cloned.1.call-update
  20.9 0.0 reduce-scatter.2.cloned.1.call-start
  20.9 0.0 copy-done.1
  20.9 0.2 copy.29
  21.1 0.3 copy.35
  21.4 53.8 %all-gather.4.cloned.1.call-done = bf16[4096,128]{1,0:T(8,128)(2,1)} async-done(((bf16[256,128]{1,0:T(8,128)(2,1)}), bf16[4096,128]{1,0:T(8,128)(2,1)}) %all-gather.4.cloned.1.call-update) | async-done | bytes 1048592 | tf_op jit(solution)/shard_map/all_gather | solution.py:44
  75.3 2.8 while.37
  75.3 0.1 broadcast_compare_fusion.6
  75.4 1.7 fusion.94
  77.1 0.9 exponential_reduce_fusion.2
  78.1 34.0 %all-gather.6.cloned.1.call-done = bf16[4096,128]{1,0:T(8,128)(2,1)} async-done(((bf16[256,128]{1,0:T(8,128)(2,1)}), bf16[4096,128]{1,0:T(8,128)(2,1)}) %all-gather.6.cloned.1.call-update) | async-done | bytes 1048592 | tf_op jit(solution)/shard_map/all_gather | solution.py:45
  112.0 0.1 broadcast.137.clone
  112.1 2.9 while.38
  112.2 0.1 broadcast_compare_fusion.7
  112.3 2.7 fusion.98
  115.0 0.2 copy.34
  115.3 0.0 all-to-all-done
  115.3 11.6 %convolution_convert_fusion = bf16[256,1024]{1,0:T(8,128)(2,1)S(1)} fusion(bf16[256,8192]{0,1:T(8,128)(2,1)} %bitcast.2, bf16[1024,8192]{1,0:T(8,128)(2,1)} %param.17), kind=kOutput, calls=%fused_computation.63 | convolution fusion | flops 4295229440 | bytes 21495808 | tf_op jit(solution)/shard_map/dot_general | solution.py:101
  126.9 0.1 copy_bitcast_fusion.1
  127.0 0.1 copy.42
  127.1 0.3 copy.32
  127.4 0.2 multiply_reduce_fusion.2
  127.6 0.1 broadcast.137
  127.7 2.2 broadcast_in_dim.48
  129.9 11.3 %while.39 = (s32[]{:T(128)}, f32[256,8,128]{2,0,1:T(8,128)S(1)}, f32[4096,256]{1,0:T(8,128)}, s32[]{:T(128)}, bf16[4096,128]{1,0:T(8,128)(2,1)}, /*index=5*/bf16...) while((s32[]{:T(128)}, f32[256,8,128]{2,0,1:T(8,128)S(1)}, ...), condition=%wide.region_8.9_spmd.clone, body=%wide.region_7.8_spmd.clone.sunk | while | flops 1354236672 | bytes 24934616 | solution.py:157
  129.9 0.1 broadcast_compare_fusion.8
  130.1 1.6 fusion.109
  131.7 2.4 fusion.110
  134.1 1.8 convolution_add_fusion.2
  136.0 2.4 fusion.111
  138.4 2.8 fusion.112
  141.2 3.8 %convert_element_type.47 = bf16[4096,256]{1,0:T(8,128)(2,1)} convert(f32[4096,256]{1,0:T(8,128)} %get-tuple-element.150) | non-fusion elementwise | flops 1048576 | bytes 6291456 | tf_op jit(solution)/shard_map/convert_element_type | solution.py:163
  145.0 0.0 reduce-scatter.2.cloned.1.call-update
  145.0 7.0 %multiply_reduce_fusion = f32[1024]{0:T(1024)S(1)} fusion(bf16[256,8192]{0,1:T(8,128)(2,1)} %bitcast.2, bf16[256,1024]{0,1:T(8,128)(2,1)S(1)} %bitcast.156), kind=kOutput, calls=%fused_computation.61 | convolution fusion | flops 4311743488 | bytes 4722688 | tf_op jit(solution)/shard_map/dot_general | solution.py:24
  152.0 0.1 bitcast_reduce_fusion
  152.1 0.5 log_bitcast_fusion
  152.6 0.1 copy_bitcast_fusion
  152.7 0.0 copy-start
  152.7 33.1 %all-gather.8.cloned.1.call-done = bf16[256,8192]{1,0:T(8,128)(2,1)} async-done(((bf16[256,1024]{1,0:T(8,128)(2,1)}), bf16[256,8192]{1,0:T(8,128)(2,1)}) %all-gather.8.cloned.1.call-update) | async-done | bytes 4194320 | tf_op jit(solution)/shard_map/all_gather | solution.py:168
  185.8 7.1 %multiply_reduce_fusion.1 = f32[1024]{0:T(1024)S(1)} fusion(bf16[256,1024]{1,0:T(8,128)(2,1)S(1)} %copy_bitcast_fusion, bf16[256,8192]{1,0:T(8,128)(2,1)} %all-gather.8.cloned.1.call-done), kind=kOutput, calls=%fused_computation.62 | convolution fusion | flops 4311743488 | bytes 4722688 | tf_op jit(solution)/shard_map/dot_general | solution.py:24
  193.0 0.0 copy-done
  193.0 0.1 bitcast_reduce_fusion.1
  193.1 0.5 log_bitcast_fusion.1
  193.6 113.3 %reduce-scatter.2.cloned.1.call-done = bf16[256,256]{1,0:T(8,128)(2,1)} async-done(((bf16[4096,256]{1,0:T(8,128)(2,1)}), bf16[256,256]{1,0:T(8,128)(2,1)}) %reduce-scatter.2.cloned.1.call-update) | async-done | bytes 131088 | tf_op jit(solution)/shard_map/reduce_scatter | solution.py:162
  307.0 1.5 fusion.57
  (12 shorter events, 0.0 us)
Async XLA Ops:
  7.2 68.1 %all-gather.4.cloned.1.call-start = ((), (), s32[]{:S(2)}) async-start(), calls=%async_computation.2 | async-start | bytes 1114112 | tf_op jit(solution)/shard_map/all_gather | solution.py:44
  7.9 104.1 %all-gather.6.cloned.1.call-start = ((), (), s32[]{:S(2)}) async-start(), calls=%async_computation.3 | async-start | bytes 1114112 | tf_op jit(solution)/shard_map/all_gather | solution.py:45
  13.0 7.9 %copy-start.1 = (bf16[256,1024]{1,0:T(8,128)(2,1)S(1)}, bf16[256,1024]{1,0:T(8,128)(2,1)}, u32[]{:S(2)}) copy-start(bf16[256,1024]{1,0:T(8,128)(2,1)} %param.14) | copy-start | bytes 1572868
  13.0 102.3 %all-to-all-start = ((bf16[8,256,1024]{1,2,0:T(8,128)(2,1)}), bf16[8,256,1024]{1,2,0:T(8,128)(2,1)}, u32[]{:S(2)}, u32[]{:S(2)}) async-start(bf16[8,256,1024]{1,2,0:T(8,128)(2,1)} %stack.2), calls=%async_computation | async-start | bytes 8388608 | tf_op jit(solution)/shard_map/all_to_all | solution.py:99
  20.1 165.7 %all-gather.8.cloned.1.call-start = ((), (), s32[]{:S(2)}) async-start(), calls=%async_computation.5 | async-start | bytes 4718592 | tf_op jit(solution)/shard_map/all_gather | solution.py:168
  20.9 286.1 %reduce-scatter.2.cloned.1.call-start = ((), (), s32[]{:S(2)}) async-start(), calls=%async_computation.4 | async-start | bytes 2228224 | tf_op jit(solution)/shard_map/reduce_scatter | solution.py:162
  152.7 40.3 %copy-start = (bf16[256,1024]{1,0:T(8,128)(2,1)}, bf16[256,1024]{1,0:T(8,128)(2,1)S(1)}, u32[]{:S(2)}) copy-start(bf16[256,1024]{1,0:T(8,128)(2,1)S(1)} %copy_bitcast_fusion) | copy-start | bytes 1572868
Sparse Core Ops, SparseCore 0:
  9.7 65.5 all-gather.3
  77.0 35.0 all-gather.5
  114.4 71.3 all-gather.7
  188.1 118.8 reduce-scatter.1
